TPU v7x, 128 devices: a whole 4x4x4 slice. The times are simulated.
128 devices in a mesh: ctx: 16 (over y, x_lo, core), head: 8 (over x_hi, z).
Axes of the slice: x: 4 (x_hi: 2, x_lo: 2; x = x_hi * 2 + x_lo), y: 4, z: 4, core: 2. Of those that a mesh axis runs over, the one named last changes fastest.
Arguments:
- queries: bfloat16 [4096, 5120], P('ctx', 'head'), may hold values from -6 to 6
- keys: bfloat16 [4096, 5120], P('ctx', 'head'), may hold values from -6 to 6
- values: bfloat16 [4096, 5120], P('ctx', 'head'), may hold values from -16 to 16
- out_weight: bfloat16 [5120, 5120], P('head'), may hold values from -0.078125 to 0.078125
- cotangent: bfloat16 [4096, 5120], P('ctx', 'head'), may hold values from -16 to 16
- contacts: int32 [32, 32], replicated, may hold values 0 or 1
- chains: int32 [32], replicated, may hold values from 0 to 3, never falling along the last dimension, each value on 1 to 16 neighbouring positions
Outputs:
- mixed: bfloat16 [4096, 5120], P('ctx', 'head')
- query_grad: bfloat16 [4096, 5120], P('ctx', 'head')
- key_grad: bfloat16 [4096, 5120], P('ctx', 'head')
- value_grad: bfloat16 [4096, 5120], P('ctx', 'head')
Inputs may be any that keep to these rules, and one draw needn't show every extreme that they name: `chains`: chain numbers never fall along the blocks; each chain has 1 to 16 blocks, one exactly 16.
All inputs are finite; a program needn't handle non-finite values.
Results may differ from a plain program's by a relative error of at most 0.02.
Values may be sent and summed in bfloat16 or wider, within the bound.
No kernel may reach another device: no remote copies, remote signals or barrier semaphores. Data moves between devices by JAX's collectives and lax.ppermute only.
A program may use at most 192 MiB of HBM per device.

v0:
```python
import jax
import jax.numpy as jnp
from jax import lax
from jax.sharding import Mesh
from jax.sharding import PartitionSpec as P

HEAD_SIZE = 128
BLOCK = 128
NEG = -1e30
CTX = ("ctxo", "core")
SWAP = [(0, 1), (1, 0)]


def swap(value):
    return lax.ppermute(value, "core", SWAP)


def pair_rows(own, other, core):
    first = jnp.where(core == 0, own, other)
    second = jnp.where(core == 0, other, own)
    return jnp.concatenate([first, second], axis=0)


def halves(value, core):
    rows = value.shape[0] // 2
    top, bottom = (value[:rows], value[rows:])
    own = jnp.where(core == 0, top, bottom)
    other = jnp.where(core == 0, bottom, top)
    return (own, other)


def per_device(queries, keys, values, out_weight, cotangent, contacts, chains):
    scale = HEAD_SIZE ** (-0.5)
    rows = queries.shape[0]
    size = HEAD_SIZE
    heads = queries.shape[1] // size
    width = heads * size
    n_out = lax.axis_size("ctxo")
    n_head = lax.axis_size("head")
    core = lax.axis_index("core")
    outer = lax.axis_index("ctxo")
    allowed = jnp.logical_or(chains[:, None] == chains[None, :], contacts > 0)
    q_blocks = rows // BLOCK
    spread = jnp.broadcast_to(cotangent[:, None, :], (rows, n_head, width))
    full_cotangent = lax.all_to_all(spread, "head", 1, 1, tiled=True).reshape(rows, n_head * width)
    grads = lax.dot_general(
        full_cotangent, out_weight, (((1,), (1,)), ((), ())), preferred_element_type=jnp.float32
    ).astype(jnp.bfloat16)
    key_half = lax.all_gather(keys, "ctxo", axis=0, tiled=True)
    value_half = lax.all_gather(values, "ctxo", axis=0, tiled=True)
    count = key_half.shape[0]
    q_chip = pair_rows(queries, swap(queries), core)
    chip_rows = 2 * rows
    q_three = q_chip.reshape(chip_rows, heads, size)
    k_three = key_half.reshape(count, heads, size)
    v_three = value_half.reshape(count, heads, size)
    row_blocks = outer * (2 * q_blocks) + jnp.arange(2 * q_blocks)
    shard = 2 * jnp.arange(n_out) + core
    col_blocks = (shard[:, None] * q_blocks + jnp.arange(q_blocks)[None, :]).reshape(-1)
    part_mask = allowed[row_blocks][:, col_blocks]
    keep = jnp.repeat(jnp.repeat(part_mask, BLOCK, axis=0), BLOCK, axis=1)[:, None, :]
    scores = (
        jnp.einsum("qhd,khd->qhk", q_three, k_three, preferred_element_type=jnp.float32) * scale
    )
    scores = jnp.where(keep, scores, NEG)
    best = jnp.max(scores, axis=2)
    weights = jnp.where(keep, jnp.exp(scores - best[:, :, None]), 0.0)
    total = jnp.sum(weights, axis=2)
    accum = jnp.einsum(
        "qhk,khd->qhd", weights.astype(jnp.bfloat16), v_three, preferred_element_type=jnp.float32
    )
    state = jnp.concatenate([best, total, accum.reshape(chip_rows, width)], axis=1)
    own_state, other_state = halves(state, core)
    got_state = swap(other_state)
    best_a, total_a, acc_a = (
        own_state[:, :heads],
        own_state[:, heads : 2 * heads],
        own_state[:, 2 * heads :],
    )
    best_b, total_b, acc_b = (
        got_state[:, :heads],
        got_state[:, heads : 2 * heads],
        got_state[:, 2 * heads :],
    )
    best_m = jnp.maximum(best_a, best_b)
    fa = jnp.exp(best_a - best_m)
    fb = jnp.exp(best_b - best_m)
    total_m = total_a * fa + total_b * fb
    acc_m = (
        acc_a.reshape(rows, heads, size) * fa[:, :, None]
        + acc_b.reshape(rows, heads, size) * fb[:, :, None]
    )
    attended = (acc_m / total_m[:, :, None]).astype(jnp.bfloat16)
    lse = best_m + jnp.log(total_m)
    projected = jnp.dot(
        attended.reshape(rows, width), out_weight, preferred_element_type=jnp.float32
    )
    parts = lax.all_to_all(
        projected.astype(jnp.bfloat16).reshape(rows, n_head, width), "head", 1, 1, tiled=True
    )
    mixed = jnp.sum(parts.astype(jnp.float32), axis=1).astype(jnp.bfloat16)
    g_own = grads.reshape(rows, heads, size)
    delta = jnp.sum(g_own.astype(jnp.float32) * attended.astype(jnp.float32), axis=2)
    side = jnp.concatenate([lse, delta], axis=1)
    side_chip = pair_rows(side, swap(side), core)
    lse_chip, delta_chip = (side_chip[:, :heads], side_chip[:, heads:])
    g_chip = pair_rows(grads, swap(grads), core).reshape(chip_rows, heads, size)
    scores = (
        jnp.einsum("qhd,khd->qhk", q_three, k_three, preferred_element_type=jnp.float32) * scale
    )
    probs = jnp.where(keep, jnp.exp(scores - lse_chip[:, :, None]), 0.0)
    dprob = jnp.einsum("qhd,khd->qhk", g_chip, v_three, preferred_element_type=jnp.float32)
    dscore = (probs * (dprob - delta_chip[:, :, None])).astype(jnp.bfloat16)
    q_part = jnp.einsum("qhk,khd->qhd", dscore, k_three, preferred_element_type=jnp.float32) * scale
    q_own, q_other = halves(q_part.reshape(chip_rows, width), core)
    query_grad = (q_own + swap(q_other)).astype(jnp.bfloat16)
    key_part = (
        jnp.einsum("qhk,qhd->khd", dscore, q_three, preferred_element_type=jnp.float32) * scale
    ).astype(jnp.bfloat16)
    value_part = jnp.einsum(
        "qhk,qhd->khd", probs.astype(jnp.bfloat16), g_chip, preferred_element_type=jnp.float32
    ).astype(jnp.bfloat16)
    key_grad = lax.psum_scatter(
        key_part.reshape(count, width), "ctxo", scatter_dimension=0, tiled=True
    )
    value_grad = lax.psum_scatter(
        value_part.reshape(count, width), "ctxo", scatter_dimension=0, tiled=True
    )
    return (mixed, query_grad, key_grad, value_grad)


def solution(mesh):
    devices = mesh.devices
    n_ctx, n_head = devices.shape
    split = Mesh(devices.reshape(n_ctx // 2, 2, n_head), ("ctxo", "core", "head"))
    rows_spec = P(CTX, "head")
    in_specs = (rows_spec, rows_spec, rows_spec, P("head", None), rows_spec, P(), P())
    out_specs = (rows_spec, rows_spec, rows_spec, rows_spec)
    return jax.shard_map(
        per_device, mesh=split, in_specs=in_specs, out_specs=out_specs, check_vma=False
    )
```

profile of v0, /device:TPU:1, one launch (start us, length us, event | category | flops | bytes accessed | tf_op | source)
XLA Modules:
  0.0 379.9 jit_solution(15274366431642683863)
XLA Ops:
  7.2 0.0 all-gather.3.cloned.1.call-start
  7.2 1.9 copy.65
  9.2 2.7 broadcast_in_dim.54
  11.9 8.3 %all-to-all-start.1 = ((bf16[256,8,640]{2,0,1:T(8,128)(2,1)}), bf16[256,8,640]{2,0,1:T(8,128)(2,1)}, u32[]{:S(2)}, u32[]{:S(2)}) async-start(bf16[256,8,640]{2,0,1:T(8,128)(2,1)} %broadcast_in_dim.54), calls=%async_computation.1 | async-start | bytes 5242880 | tf_op jit(solution)/shard_map/all_to_all | solution.py:45
  20.2 0.0 all-gather.5.cloned.1.call-start
  20.3 0.7 all-gather.5.cloned.1.call-update
  21.0 0.0 reduce-scatter.3.cloned.1.call-start
  21.0 1.0 collective-permute-start
  22.1 0.1 compare_or_fusion
  22.2 0.6 gather_fusion
  22.7 0.1 copy.62
  22.8 0.1 iota_add_fusion
  22.9 0.1 add.94
  23.0 0.6 gather_fusion.1
  23.6 0.1 copy.63
  23.7 3.5 broadcast_in_dim.49
  27.2 0.6 copy.87
  27.8 0.1 broadcast_select_fusion.3
  27.9 0.1 pad_maximum_fusion.1
  28.0 1.2 copy.64
  29.2 48.6 %all-to-all-done.1 = bf16[256,8,640]{2,0,1:T(8,128)(2,1)} async-done(((bf16[256,8,640]{2,0,1:T(8,128)(2,1)}), bf16[256,8,640]{2,0,1:T(8,128)(2,1)}, u32[]{:S(2)}, u32[]{:S(2)}) %all-to-all-start.1) | async-done | bytes 2621472 | tf_op jit(solution)/shard_map/all_to_all | solution.py:45
  77.8 4.4 %copy.70 = bf16[256,8,640]{0,2,1:T(8,128)(2,1)} copy(bf16[256,8,640]{2,0,1:T(8,128)(2,1)} %all-to-all-done.1) | data formatting | bytes 5242880 | tf_op jit(solution)/shard_map/all_to_all | solution.py:45
  82.2 16.7 %all-gather.3.cloned.1.call-done = bf16[2048,640]{0,1:T(8,128)(2,1)} async-done(((bf16[256,640]{0,1:T(8,128)(2,1)}), bf16[2048,640]{0,1:T(8,128)(2,1)}) %all-gather.3.cloned.1.call-update) | async-done | bytes 2621456 | tf_op jit(solution)/shard_map/all_gather | solution.py:49
  98.9 6.1 %fusion.4 = (f32[512,5]{0,1:T(8,128)S(1)}, f32[5,512,2048]{2,1,0:T(8,128)S(1)}) fusion(pred[512,2048]{1,0:T(8,128)(4,1)S(1)} %bitcast.92, bf16[512,5,128]{0,2,1:T(8,128)(2,1)} %bitcast.100, bf16[2048,5,128]{0,2,1:T(8,128)(2,1)} %bitcast.102), kind=kOutput, calls=%fused_computation.10 | convolution fusion | flops 1357903360 | bytes 25307136 | tf_op jit(solution)/shard_map/qhd,khd->qhk/dot_general | solution.py:63
  105.1 7.0 %copy-done = f32[5,512,2048]{2,1,0:T(8,128)} copy-done((f32[5,512,2048]{2,1,0:T(8,128)}, f32[5,512,2048]{2,1,0:T(8,128)S(1)}, u32[]{:S(2)}) %copy-start) | copy-done | bytes 20971544
  112.1 6.7 %fusion.7 = f32[512,5]{0,1:T(8,128)S(1)} fusion(f32[5,512,2048]{2,1,0:T(8,128)S(1)} %get-tuple-element.24, f32[512,5]{0,1:T(8,128)S(1)} %get-tuple-element.23, pred[512,2048]{1,0:T(8,128)(4,1)S(1)} %bitcast.93), kind=kLoop, calls=%fused_computation.13 | loop fusion | flops 26211840 | bytes 22040576 | tf_op jit(solution)/shard_map/reduce_sum | solution.py:68
  118.8 45.7 %all-gather.5.cloned.1.call-done = bf16[2048,640]{1,0:T(8,128)(2,1)} async-done(((bf16[256,640]{1,0:T(8,128)(2,1)}), bf16[2048,640]{1,0:T(8,128)(2,1)}) %all-gather.5.cloned.1.call-update) | async-done | bytes 2621456 | tf_op jit(solution)/shard_map/all_gather | solution.py:50
  164.5 4.5 %copy.68 = bf16[2048,640]{0,1:T(8,128)(2,1)} copy(bf16[2048,640]{1,0:T(8,128)(2,1)} %all-gather.5.cloned.1.call-done) | data formatting | bytes 5242880 | tf_op jit(solution)/shard_map/all_gather | solution.py:50
  169.0 11.1 %fusion.10 = f32[5,512,128]{1,2,0:T(8,128)S(1)} fusion(bf16[2048,5,128]{0,2,1:T(8,128)(2,1)} %bitcast.105, f32[5,512,2048]{2,1,0:T(8,128)} %copy-done, f32[512,5]{0,1:T(8,128)S(1)} %get-tuple-element.23, pred[512,2048]{1,0:T(8,128)(4,1)S(1)} %bitcast.94), kind=kOutput, calls=%fused_computation.15 | convolution fusion | flops 1368391680 | bytes 25962496 | tf_op jit(solution)/shard_map/qhk,khd->qhd/dot_general | solution.py:69
  180.0 0.2 pad_maximum_fusion
  180.2 1.0 slice_select_fusion.1
  181.2 1.2 collective-permute-start.1
  182.3 5.2 %convolution_convert_fusion.1 = bf16[256,640]{1,0:T(8,128)(2,1)S(1)} fusion(bf16[256,5120]{0,1:T(8,128)(2,1)S(1)} %bitcast.107, bf16[640,5120]{1,0:T(8,128)(2,1)} %param.10), kind=kOutput, calls=%fused_computation.26 | convolution fusion | flops 1677885440 | bytes 9502720 | tf_op jit(solution)/shard_map/dot_general | solution.py:46
  187.5 0.1 collective-permute-start.3
  187.6 0.2 copy.71
  187.8 1.4 collective-permute-done.3
  189.2 0.1 broadcast_select_fusion.1
  189.3 0.8 log_add_fusion
  190.1 1.3 fusion.30
  191.4 0.2 multiply_reduce_fusion
  191.6 0.2 collective-permute-start.2
  191.8 0.1 pad_maximum_fusion.2
  191.9 0.3 copy.72
  192.1 0.7 collective-permute-done.2
  192.9 15.5 %fusion.1 = bf16[512,5,2048]{2,0,1:T(8,128)(2,1)} fusion(f32[5,512,2048]{2,1,0:T(8,128)} %copy-done, f32[512,5]{0,1:T(8,128)S(1)} %get-tuple-element.20, f32[512,5]{0,1:T(8,128)S(1)} %get-tuple-element.19, pred[512,2048]{1,0:T(8,128)(4,1)S(1)} %bitcast.95, bf16[512,5,128]{0,2,1:T(8,128)(2,1)S(1)} %bitcast.115, bf16[2048,5,128]{0,2,1:T(8,128)(2,1)} %bitcast.106), kind=kOutput, calls=%fused_computation.4 | convolution fusion | flops 1373634560 | bytes 35803136 | tf_op jit(solution)/shard_map/qhd,khd->qhk/dot_general | solution.py:112
  208.4 7.1 %multiply_convert_fusion = bf16[5,128,2048]{2,1,0:T(8,128)(2,1)} fusion(bf16[512,5,128]{0,2,1:T(8,128)(2,1)S(1)} %bitcast.101, bf16[512,5,2048]{2,0,1:T(8,128)(2,1)} %fusion.1), kind=kOutput, calls=%fused_computation.19 | convolution fusion | flops 1344798720 | bytes 13762560 | tf_op jit(solution)/shard_map/qhk,qhd->khd/dot_general | solution.py:118
  215.6 4.4 %copy.77 = bf16[2048,640]{1,0:T(8,128)(2,1)} copy(bf16[2048,640]{0,1:T(8,128)(2,1)} %bitcast.97) | data formatting | bytes 5242880 | tf_op jit(solution)/shard_map/reshape | solution.py:124
  220.0 0.0 reduce-scatter.3.cloned.1.call-update
  220.0 0.3 reduce-scatter.5.cloned.1.call-start
  220.3 11.4 %fusion.14 = bf16[5,128,2048]{2,1,0:T(8,128)(2,1)} fusion(bf16[512,5,128]{0,2,1:T(8,128)(2,1)S(1)} %bitcast.116, f32[5,512,2048]{2,1,0:T(8,128)} %copy-done, f32[512,5]{0,1:T(8,128)S(1)} %get-tuple-element.19, pred[512,2048]{1,0:T(8,128)(4,1)S(1)} %bitcast.96), kind=kOutput, calls=%fused_computation.21 | convolution fusion | flops 1364459520 | bytes 25307136 | tf_op jit(solution)/shard_map/qhk,qhd->khd/dot_general | solution.py:120
  231.7 4.4 %copy.78 = bf16[2048,640]{1,0:T(8,128)(2,1)} copy(bf16[2048,640]{0,1:T(8,128)(2,1)} %bitcast.108) | data formatting | bytes 5242880 | tf_op jit(solution)/shard_map/reshape | solution.py:127
  236.1 5.1 %convolution_convert_fusion = bf16[256,5120]{1,0:T(8,128)(2,1)S(1)} fusion(bf16[256,640]{0,1:T(8,128)(2,1)S(1)} %get-tuple-element.13, bf16[640,5120]{1,0:T(8,128)(2,1)} %param.10), kind=kOutput, calls=%fused_computation.18 | convolution fusion | flops 1679032320 | bytes 9502720 | tf_op jit(solution)/shard_map/dot_general | solution.py:95
  241.2 1.8 copy.88
  243.0 6.3 %all-to-all-start = ((bf16[256,8,640]{2,0,1:T(8,128)(2,1)}), bf16[256,8,640]{2,0,1:T(8,128)(2,1)S(1)}, u32[]{:S(2)}, u32[]{:S(2)}) async-start(bf16[256,8,640]{2,0,1:T(8,128)(2,1)} %bitcast.98), calls=%async_computation | async-start | bytes 5242880 | tf_op jit(solution)/shard_map/all_to_all | solution.py:98
  249.3 8.4 %fusion.17 = f32[512,5,128]{0,2,1:T(8,128)S(1)} fusion(bf16[512,5,2048]{2,0,1:T(8,128)(2,1)} %fusion.1, bf16[2048,5,128]{0,2,1:T(8,128)(2,1)} %bitcast.103), kind=kOutput, calls=%fused_computation.24 | convolution fusion | flops 1342504960 | bytes 14417920 | tf_op jit(solution)/shard_map/qhk,khd->qhd/dot_general | solution.py:114
  257.7 1.0 slice_select_fusion.2
  258.6 1.1 copy.75
  259.7 0.4 collective-permute-start.4
  260.2 1.3 copy.76
  261.5 0.7 collective-permute-done.4
  262.2 1.9 add_convert_fusion
  264.1 44.2 %all-to-all-done = bf16[256,8,640]{2,0,1:T(8,128)(2,1)S(1)} async-done(((bf16[256,8,640]{2,0,1:T(8,128)(2,1)}), bf16[256,8,640]{2,0,1:T(8,128)(2,1)S(1)}, u32[]{:S(2)}, u32[]{:S(2)}) %all-to-all-start) | async-done | bytes 2621472 | tf_op jit(solution)/shard_map/all_to_all | solution.py:98
  308.3 1.2 reduce_sum.31
  309.4 64.0 %reduce-scatter.5.cloned.1.call-done = bf16[256,640]{1,0:T(8,128)(2,1)} async-done(((bf16[2048,640]{1,0:T(8,128)(2,1)}), bf16[256,640]{1,0:T(8,128)(2,1)}) %reduce-scatter.5.cloned.1.call-update) | async-done | bytes 327696 | tf_op jit(solution)/shard_map/reduce_scatter | solution.py:126
  (25 shorter events, 0.1 us)
Async XLA Ops:
  7.2 13.9 %copy-start.3 = (bf16[256,640]{1,0:T(8,128)(2,1)S(1)}, bf16[256,640]{1,0:T(8,128)(2,1)}, u32[]{:S(2)}) copy-start(bf16[256,640]{1,0:T(8,128)(2,1)} %param.7) | copy-start | bytes 983044
  7.2 14.9 %copy-start.4 = (s32[32,32]{1,0:T(8,128)S(1)}, s32[32,32]{1,0:T(8,128)}, u32[]{:S(2)}) copy-start(s32[32,32]{1,0:T(8,128)} %param.12) | copy-start | bytes 12292
  7.2 14.9 %copy-start.5 = (s32[32]{0:T(128)S(1)}, s32[32]{0:T(128)}, u32[]{:S(2)}) copy-start(s32[32]{0:T(128)} %param.13) | copy-start | bytes 388
  7.2 91.7 %all-gather.3.cloned.1.call-start = ((), (), s32[]{:S(2)}) async-start(), calls=%async_computation.4 | async-start | bytes 2949120 | tf_op jit(solution)/shard_map/all_gather | solution.py:49
  11.9 65.9 %all-to-all-start.1 = ((bf16[256,8,640]{2,0,1:T(8,128)(2,1)}), bf16[256,8,640]{2,0,1:T(8,128)(2,1)}, u32[]{:S(2)}, u32[]{:S(2)}) async-start(bf16[256,8,640]{2,0,1:T(8,128)(2,1)} %broadcast_in_dim.54), calls=%async_computation.1 | async-start | bytes 5242880 | tf_op jit(solution)/shard_map/all_to_all | solution.py:45
  20.2 144.3 %all-gather.5.cloned.1.call-start = ((), (), s32[]{:S(2)}) async-start(), calls=%async_computation.5 | async-start | bytes 2949120 | tf_op jit(solution)/shard_map/all_gather | solution.py:50
  21.0 288.5 %reduce-scatter.3.cloned.1.call-start = ((), (), s32[]{:S(2)}) async-start(), calls=%async_computation.6 | async-start | bytes 2949120 | tf_op jit(solution)/shard_map/reduce_scatter | solution.py:123
  21.0 6.8 %collective-permute-start = (bf16[256,640]{1,0:T(8,128)(2,1)S(1)}, bf16[256,640]{1,0:T(8,128)(2,1)S(1)}, u32[]{:S(2)}, u32[]{:S(2)}) collective-permute-start(bf16[256,640]{1,0:T(8,128)(2,1)S(1)} %copy-done.3), channel_id=1, source_target_pairs={{0,8},{8,0},{1,9},{9,1},{2,10},{10,2},{3,11},{11,3},{4,12},{12,4},... | collective-permute-start | bytes 983048 | tf_op jit(solution)/shard_map/ppermute | solution.py:15
  105.1 7.0 %copy-start = (f32[5,512,2048]{2,1,0:T(8,128)}, f32[5,512,2048]{2,1,0:T(8,128)S(1)}, u32[]{:S(2)}) copy-start(f32[5,512,2048]{2,1,0:T(8,128)S(1)} %get-tuple-element.24) | copy-start | bytes 62914564
  169.0 13.4 %copy-start.2 = (bf16[256,8,640]{0,2,1:T(8,128)(2,1)S(1)}, bf16[256,8,640]{0,2,1:T(8,128)(2,1)}, u32[]{:S(2)}) copy-start(bf16[256,8,640]{0,2,1:T(8,128)(2,1)} %copy.70) | copy-start | bytes 7864324
  181.2 8.2 %collective-permute-start.1 = (f32[256,650]{0,1:T(8,128)}, f32[256,650]{0,1:T(8,128)}, u32[]{:S(2)}, u32[]{:S(2)}) collective-permute-start(f32[256,650]{0,1:T(8,128)} %get-tuple-element.9), channel_id=1, source_target_pairs={{0,8},{8,0},{1,9},{9,1},{2,10},{10,2},{3,11},{11,3},{4,12},{12,4},... | collective-permute-start | bytes 1996808 | tf_op jit(solution)/shard_map/ppermute | solution.py:15
  187.5 1.7 collective-permute-start.3
  191.6 1.3 collective-permute-start.2
  192.9 15.5 %copy-start.1 = (bf16[512,640]{0,1:T(8,128)(2,1)S(1)}, bf16[512,640]{0,1:T(8,128)(2,1)}, u32[]{:S(2)}) copy-start(bf16[512,640]{0,1:T(8,128)(2,1)} %copy.64) | copy-start | bytes 1966084
  220.0 153.4 %reduce-scatter.5.cloned.1.call-start = ((), (), s32[]{:S(2)}) async-start(), calls=%async_computation.7 | async-start | bytes 2949120 | tf_op jit(solution)/shard_map/reduce_scatter | solution.py:126
  243.0 65.3 %all-to-all-start = ((bf16[256,8,640]{2,0,1:T(8,128)(2,1)}), bf16[256,8,640]{2,0,1:T(8,128)(2,1)S(1)}, u32[]{:S(2)}, u32[]{:S(2)}) async-start(bf16[256,8,640]{2,0,1:T(8,128)(2,1)} %bitcast.98), calls=%async_computation | async-start | bytes 5242880 | tf_op jit(solution)/shard_map/all_to_all | solution.py:98
  259.7 2.5 collective-permute-start.4
Sparse Core Ops, SparseCore 0:
  10.1 88.7 all-gather.2
  100.6 63.8 all-gather.4
  220.1 88.7 reduce-scatter.2
  311.7 61.6 reduce-scatter.4
where the time goes:
time: 381 us; the launch traced here: 380 us
  waiting for transfers between devices  223 us (59%)
  matrix products  69.9 us (18%)
  local copies, waits for them, and re-layouts  40.7 us (11%)
  starting transfers between devices  17.9 us (5%)
  other arithmetic  14.6 us (4%)
  between operations  14 us (4%)
    reduce_scatter x1, waiting for transfers between devices, per_device(): lax.psum_scatter(value_part.reshape(count, width), 'ctxo', scatter_dimens...  64 us
    all_to_all x1, waiting for transfers between devices, per_device(): lax.all_to_all(spread, 'head', 1, 1, tiled=True)  48.6 us
    all_gather x1, waiting for transfers between devices, per_device(): value_half = lax.all_gather(values, 'ctxo', axis=0, tiled=True)  45.7 us
    all_to_all x1, waiting for transfers between devices, per_device(): lax.all_to_all(projected.astype(jnp.bfloat16).reshape(rows, n_head, width...  44.2 us
    all_gather x1, waiting for transfers between devices, per_device(): key_half = lax.all_gather(keys, 'ctxo', axis=0, tiled=True)  16.7 us
    dot_general x1, matrix products, per_device(): jnp.einsum('qhd,khd->qhk', g_chip, v_three, preferred_element_type=jnp.fl...  15.5 us
    dot_general x1, matrix products, per_device(): jnp.einsum('qhk,qhd->khd', probs.astype(jnp.bfloat16), g_chip, preferred_...  11.4 us
    dot_general x1, matrix products, per_device(): jnp.einsum('qhk,khd->qhd', weights.astype(jnp.bfloat16), v_three, preferr...  11.1 us
  transfers between devices with their start and end apart: 11, of which 8 were waited for; matrix products, arithmetic and copies ran while one was open for 18% of the time, Pallas kernels for 0%

commit v1 on v0

--- a/solution.py
+++ b/solution.py
@@ -46,7 +46,8 @@
     grads = lax.dot_general(
         full_cotangent, out_weight, (((1,), (1,)), ((), ())), preferred_element_type=jnp.float32
     ).astype(jnp.bfloat16)
-    key_half = lax.all_gather(keys, "ctxo", axis=0, tiled=True)
+    sent = jnp.stack([keys] * lax.axis_size("ctxo"))
+    key_half = jnp.concatenate(lax.all_to_all(sent, "ctxo", 0, 0), axis=0)
     value_half = lax.all_gather(values, "ctxo", axis=0, tiled=True)
     count = key_half.shape[0]
     q_chip = pair_rows(queries, swap(queries), core)

time: 381 us -> 353 us (0.927)
  waiting for transfers between devices: 223 us -> 150 us
  blocking collectives: 0 us -> 38.1 us
  local copies, waits for them, and re-layouts: 40.7 us -> 47 us
    all_to_all x0 -> x1, blocking collectives: none -> 38.1 us  [per_device(): key_half = jnp.concatenate(lax.all_to_all(sent, 'ctxo', 0, 0), axis=0)]
    all_gather x1, waiting for transfers between devices: 45.7 us -> 10.6 us  [per_device(): value_half = lax.all_gather(values, 'ctxo', axis=0, tiled=True)]
    all_to_all x1, waiting for transfers between devices: 48.6 us -> 24.1 us  [per_device(): lax.all_to_all(spread, 'head', 1, 1, tiled=True)]
    all_gather x1 -> x0, waiting for transfers between devices: 16.7 us -> none  [per_device(): key_half = lax.all_gather(keys, 'ctxo', axis=0, tiled=True)]
    another operation x0 -> x2, local copies, waits for them, and re-layouts: none -> 5.42 us  [the longest x1 5.25 us: per_device(): k_three = key_half.reshape(count, heads, size)]
    all_to_all x1, waiting for transfers between devices: 44.2 us -> 48.9 us  [per_device(): lax.all_to_all(projected.astype(jnp.bfloat16).reshape(rows, n_head, width...]
    all_to_all x0 -> x1, local copies, waits for them, and re-layouts: none -> 4.74 us  [per_device(): key_half = jnp.concatenate(lax.all_to_all(sent, 'ctxo', 0, 0), axis=0)]
    unnamed x14 -> x18, local copies, waits for them, and re-layouts: 9.6 us -> 8.88 us
  transfers between devices with their start and end apart: 11 -> 10, of which waited for: 8 -> 7; matrix products, arithmetic and copies ran while one was open for 18% -> 21% of each run, Pallas kernels for 0% -> 0%
where the time goes in v1:
time: 353 us; the launch traced here: 352 us
  waiting for transfers between devices  150 us (42%)
  matrix products  69.2 us (20%)
  local copies, waits for them, and re-layouts  47 us (13%)
  blocking collectives  38.1 us (11%)
  starting transfers between devices  18.5 us (5%)
  other arithmetic  14.3 us (4%)
  between operations  14 us (4%)
    reduce_scatter x1, waiting for transfers between devices, per_device(): lax.psum_scatter(value_part.reshape(count, width), 'ctxo', scatter_dimens...  62.4 us
    all_to_all x1, waiting for transfers between devices, per_device(): lax.all_to_all(projected.astype(jnp.bfloat16).reshape(rows, n_head, width...  48.9 us
    all_to_all x1, blocking collectives, per_device(): key_half = jnp.concatenate(lax.all_to_all(sent, 'ctxo', 0, 0), axis=0)  38.1 us
    all_to_all x1, waiting for transfers between devices, per_device(): lax.all_to_all(spread, 'head', 1, 1, tiled=True)  24.1 us
    dot_general x1, matrix products, per_device(): jnp.einsum('qhd,khd->qhk', g_chip, v_three, preferred_element_type=jnp.fl...  15.5 us
    dot_general x1, matrix products, per_device(): jnp.einsum('qhk,qhd->khd', probs.astype(jnp.bfloat16), g_chip, preferred_...  11.4 us
    dot_general x1, matrix products, per_device(): jnp.einsum('qhk,khd->qhd', weights.astype(jnp.bfloat16), v_three, preferr...  11.1 us
    all_gather x1, waiting for transfers between devices, per_device(): value_half = lax.all_gather(values, 'ctxo', axis=0, tiled=True)  10.6 us
  transfers between devices with their start and end apart: 10, of which 7 were waited for; matrix products, arithmetic and copies ran while one was open for 21% of the time, Pallas kernels for 0%

profile of v1, /device:TPU:1, one launch (start us, length us, event | category | flops | bytes accessed | tf_op | source)
XLA Modules:
  0.0 351.6 jit_solution(14120095099473241417)
XLA Ops:
  7.2 1.2 copy.66
  8.4 0.2 stack.2
  8.6 38.1 %all_to_all.15 = bf16[8,256,640]{1,2,0:T(8,128)(2,1)} all-to-all(bf16[8,256,640]{1,2,0:T(8,128)(2,1)S(1)} %stack.2), channel_id=1, replica_groups=mesh['ctxo'=8,'core'=2,'head'=8] {'ctxo'}, dimensions={0} | all-to-all | bytes 5242880 | tf_op jit(solution)/shard_map/all_to_all | solution.py:50
  46.6 1.7 broadcast_in_dim.54
  48.3 7.2 %all-to-all-start.2 = ((bf16[256,8,640]{2,0,1:T(8,128)(2,1)}), bf16[256,8,640]{2,0,1:T(8,128)(2,1)}, u32[]{:S(2)}, u32[]{:S(2)}) async-start(bf16[256,8,640]{2,0,1:T(8,128)(2,1)} %broadcast_in_dim.54), calls=%async_computation.2 | async-start | bytes 5242880 | tf_op jit(solution)/shard_map/all_to_all | solution.py:45
  55.6 0.7 all-gather.2.cloned.1.call-update
  56.3 0.0 reduce-scatter.3.cloned.1.call-start
  56.3 2.2 collective-permute-start
  58.5 0.1 compare_or_fusion
  58.6 0.6 gather_fusion
  59.2 0.1 copy.63
  59.3 0.1 iota_add_fusion
  59.3 0.1 add.94
  59.4 0.6 gather_fusion.1
  60.0 0.1 copy.64
  60.1 3.5 broadcast_in_dim.49
  63.6 0.6 copy.89
  64.3 0.1 broadcast_select_fusion.3
  64.3 0.1 pad_maximum_fusion.1
  64.4 1.1 copy.65
  65.6 4.7 %copy.67 = bf16[8,256,640]{1,0,2:T(8,128)(2,1)} copy(bf16[8,256,640]{1,2,0:T(8,128)(2,1)} %all_to_all.15) | data formatting | bytes 5242880 | tf_op jit(solution)/shard_map/all_to_all | solution.py:50
  70.3 5.2 %reshape_reshape.3 = bf16[2048,5,128]{0,2,1:T(8,128)(2,1)} reshape(bf16[8,256,640]{1,0,2:T(8,128)(2,1)} %copy.67) | data formatting | bytes 5242880 | tf_op jit(solution)/shard_map/reshape;reshape | solution.py:56
  75.5 24.1 %all-to-all-done.2 = bf16[256,8,640]{2,0,1:T(8,128)(2,1)} async-done(((bf16[256,8,640]{2,0,1:T(8,128)(2,1)}), bf16[256,8,640]{2,0,1:T(8,128)(2,1)}, u32[]{:S(2)}, u32[]{:S(2)}) %all-to-all-start.2) | async-done | bytes 2621472 | tf_op jit(solution)/shard_map/all_to_all | solution.py:45
  99.6 4.4 %copy.72 = bf16[256,8,640]{0,2,1:T(8,128)(2,1)} copy(bf16[256,8,640]{2,0,1:T(8,128)(2,1)} %all-to-all-done.2) | data formatting | bytes 5242880 | tf_op jit(solution)/shard_map/all_to_all | solution.py:45
  104.0 6.1 %fusion.4 = (f32[512,5]{0,1:T(8,128)S(1)}, f32[5,512,2048]{2,1,0:T(8,128)S(1)}) fusion(pred[512,2048]{1,0:T(8,128)(4,1)S(1)} %bitcast.93, bf16[512,5,128]{0,2,1:T(8,128)(2,1)} %bitcast.101, bf16[2048,5,128]{0,2,1:T(8,128)(2,1)} %reshape_reshape.3), kind=kOutput, calls=%fused_computation.10 | convolution fusion | flops 1357903360 | bytes 25307136 | tf_op jit(solution)/shard_map/qhd,khd->qhk/dot_general | solution.py:64
  110.2 7.0 %copy-done = f32[5,512,2048]{2,1,0:T(8,128)} copy-done((f32[5,512,2048]{2,1,0:T(8,128)}, f32[5,512,2048]{2,1,0:T(8,128)S(1)}, u32[]{:S(2)}) %copy-start) | copy-done | bytes 20971544
  117.2 6.7 %fusion.7 = f32[512,5]{0,1:T(8,128)S(1)} fusion(f32[5,512,2048]{2,1,0:T(8,128)S(1)} %get-tuple-element.24, f32[512,5]{0,1:T(8,128)S(1)} %get-tuple-element.23, pred[512,2048]{1,0:T(8,128)(4,1)S(1)} %bitcast.94), kind=kLoop, calls=%fused_computation.13 | loop fusion | flops 26211840 | bytes 22040576 | tf_op jit(solution)/shard_map/reduce_sum | solution.py:69
  123.9 10.6 %all-gather.2.cloned.1.call-done = bf16[2048,640]{1,0:T(8,128)(2,1)} async-done(((bf16[256,640]{1,0:T(8,128)(2,1)}), bf16[2048,640]{1,0:T(8,128)(2,1)}) %all-gather.2.cloned.1.call-update) | async-done | bytes 2621456 | tf_op jit(solution)/shard_map/all_gather | solution.py:51
  134.5 4.5 %copy.70 = bf16[2048,640]{0,1:T(8,128)(2,1)} copy(bf16[2048,640]{1,0:T(8,128)(2,1)} %all-gather.2.cloned.1.call-done) | data formatting | bytes 5242880 | tf_op jit(solution)/shard_map/all_gather | solution.py:51
  139.0 11.1 %fusion.10 = f32[5,512,128]{1,2,0:T(8,128)S(1)} fusion(bf16[2048,5,128]{0,2,1:T(8,128)(2,1)} %bitcast.104, f32[5,512,2048]{2,1,0:T(8,128)} %copy-done, f32[512,5]{0,1:T(8,128)S(1)} %get-tuple-element.23, pred[512,2048]{1,0:T(8,128)(4,1)S(1)} %bitcast.95), kind=kOutput, calls=%fused_computation.15 | convolution fusion | flops 1368391680 | bytes 25962496 | tf_op jit(solution)/shard_map/qhk,khd->qhd/dot_general | solution.py:70
  150.1 0.2 pad_maximum_fusion
  150.2 1.0 slice_select_fusion.1
  151.2 0.6 collective-permute-start.1
  151.8 5.2 %convolution_convert_fusion.1 = bf16[256,640]{1,0:T(8,128)(2,1)S(1)} fusion(bf16[256,5120]{0,1:T(8,128)(2,1)S(1)} %bitcast.106, bf16[640,5120]{1,0:T(8,128)(2,1)} %param.10), kind=kOutput, calls=%fused_computation.26 | convolution fusion | flops 1677885440 | bytes 9502720 | tf_op jit(solution)/shard_map/dot_general | solution.py:46
  157.0 0.1 collective-permute-start.3
  157.1 0.2 copy.73
  157.2 1.4 collective-permute-done.3
  158.7 0.1 broadcast_select_fusion.1
  158.8 0.8 log_add_fusion
  159.6 1.3 fusion.30
  160.9 0.2 multiply_reduce_fusion
  161.1 0.2 collective-permute-start.2
  161.3 0.1 pad_maximum_fusion.2
  161.3 0.3 copy.74
  161.6 0.7 collective-permute-done.2
  162.4 15.5 %fusion.1 = bf16[512,5,2048]{2,0,1:T(8,128)(2,1)} fusion(f32[5,512,2048]{2,1,0:T(8,128)} %copy-done, f32[512,5]{0,1:T(8,128)S(1)} %get-tuple-element.20, f32[512,5]{0,1:T(8,128)S(1)} %get-tuple-element.19, pred[512,2048]{1,0:T(8,128)(4,1)S(1)} %bitcast.96, bf16[512,5,128]{0,2,1:T(8,128)(2,1)S(1)} %bitcast.114, bf16[2048,5,128]{0,2,1:T(8,128)(2,1)} %bitcast.105), kind=kOutput, calls=%fused_computation.4 | convolution fusion | flops 1373634560 | bytes 35803136 | tf_op jit(solution)/shard_map/qhd,khd->qhk/dot_general | solution.py:113
  177.9 7.1 %multiply_convert_fusion = bf16[5,128,2048]{2,1,0:T(8,128)(2,1)} fusion(bf16[512,5,128]{0,2,1:T(8,128)(2,1)S(1)} %bitcast.102, bf16[512,5,2048]{2,0,1:T(8,128)(2,1)} %fusion.1), kind=kOutput, calls=%fused_computation.19 | convolution fusion | flops 1344798720 | bytes 13762560 | tf_op jit(solution)/shard_map/qhk,qhd->khd/dot_general | solution.py:119
  185.0 4.4 %copy.79 = bf16[2048,640]{1,0:T(8,128)(2,1)} copy(bf16[2048,640]{0,1:T(8,128)(2,1)} %bitcast.98) | data formatting | bytes 5242880 | tf_op jit(solution)/shard_map/reshape | solution.py:125
  189.4 0.3 reduce-scatter.5.cloned.1.call-start
  189.7 11.4 %fusion.14 = bf16[5,128,2048]{2,1,0:T(8,128)(2,1)} fusion(bf16[512,5,128]{0,2,1:T(8,128)(2,1)S(1)} %bitcast.115, f32[5,512,2048]{2,1,0:T(8,128)} %copy-done, f32[512,5]{0,1:T(8,128)S(1)} %get-tuple-element.19, pred[512,2048]{1,0:T(8,128)(4,1)S(1)} %bitcast.97), kind=kOutput, calls=%fused_computation.21 | convolution fusion | flops 1364459520 | bytes 25307136 | tf_op jit(solution)/shard_map/qhk,qhd->khd/dot_general | solution.py:121
  201.1 4.4 %copy.80 = bf16[2048,640]{1,0:T(8,128)(2,1)} copy(bf16[2048,640]{0,1:T(8,128)(2,1)} %bitcast.107) | data formatting | bytes 5242880 | tf_op jit(solution)/shard_map/reshape | solution.py:128
  205.5 5.1 %convolution_convert_fusion = bf16[256,5120]{1,0:T(8,128)(2,1)S(1)} fusion(bf16[256,640]{0,1:T(8,128)(2,1)S(1)} %get-tuple-element.13, bf16[640,5120]{1,0:T(8,128)(2,1)} %param.10), kind=kOutput, calls=%fused_computation.18 | convolution fusion | flops 1679032320 | bytes 9502720 | tf_op jit(solution)/shard_map/dot_general | solution.py:96
  210.7 1.7 copy.90
  212.4 7.4 %all-to-all-start.1 = ((bf16[256,8,640]{2,0,1:T(8,128)(2,1)}), bf16[256,8,640]{2,0,1:T(8,128)(2,1)}, u32[]{:S(2)}, u32[]{:S(2)}) async-start(bf16[256,8,640]{2,0,1:T(8,128)(2,1)} %bitcast.99), calls=%async_computation.1 | async-start | bytes 5242880 | tf_op jit(solution)/shard_map/all_to_all | solution.py:99
  219.8 7.6 %fusion.17 = f32[512,5,128]{0,2,1:T(8,128)S(1)} fusion(bf16[512,5,2048]{2,0,1:T(8,128)(2,1)} %fusion.1, bf16[2048,5,128]{0,2,1:T(8,128)(2,1)S(1)} %copy-done.1), kind=kOutput, calls=%fused_computation.24 | convolution fusion | flops 1342504960 | bytes 14417920 | tf_op jit(solution)/shard_map/qhk,khd->qhd/dot_general | solution.py:115
  227.5 0.1 slice_select_fusion.2
  227.6 0.2 copy.77
  227.8 0.5 collective-permute-start.4
  228.3 0.2 copy.78
  228.6 1.5 collective-permute-done.4
  230.0 0.8 add_convert_fusion
  230.8 48.9 %all-to-all-done.1 = bf16[256,8,640]{2,0,1:T(8,128)(2,1)} async-done(((bf16[256,8,640]{2,0,1:T(8,128)(2,1)}), bf16[256,8,640]{2,0,1:T(8,128)(2,1)}, u32[]{:S(2)}, u32[]{:S(2)}) %all-to-all-start.1) | async-done | bytes 2621472 | tf_op jit(solution)/shard_map/all_to_all | solution.py:99
  279.8 2.9 reduce_sum.31
  282.7 62.4 %reduce-scatter.5.cloned.1.call-done = bf16[256,640]{1,0:T(8,128)(2,1)} async-done(((bf16[2048,640]{1,0:T(8,128)(2,1)}), bf16[256,640]{1,0:T(8,128)(2,1)}) %reduce-scatter.5.cloned.1.call-update) | async-done | bytes 327696 | tf_op jit(solution)/shard_map/reduce_scatter | solution.py:127
  (30 shorter events, 0.2 us)
Async XLA Ops:
  7.2 39.5 %copy-start.5 = (bf16[256,640]{1,0:T(8,128)(2,1)S(1)}, bf16[256,640]{1,0:T(8,128)(2,1)}, u32[]{:S(2)}) copy-start(bf16[256,640]{1,0:T(8,128)(2,1)} %param.11) | copy-start | bytes 983044
  8.5 47.8 %copy-start.4 = (bf16[256,640]{1,0:T(8,128)(2,1)S(1)}, bf16[256,640]{1,0:T(8,128)(2,1)}, u32[]{:S(2)}) copy-start(bf16[256,640]{1,0:T(8,128)(2,1)} %param.7) | copy-start | bytes 983044
  8.6 49.9 %copy-start.6 = (s32[32,32]{1,0:T(8,128)S(1)}, s32[32,32]{1,0:T(8,128)}, u32[]{:S(2)}) copy-start(s32[32,32]{1,0:T(8,128)} %param.12) | copy-start | bytes 12292
  8.6 49.9 %copy-start.7 = (s32[32]{0:T(128)S(1)}, s32[32]{0:T(128)}, u32[]{:S(2)}) copy-start(s32[32]{0:T(128)} %param.13) | copy-start | bytes 388
  48.3 51.3 %all-to-all-start.2 = ((bf16[256,8,640]{2,0,1:T(8,128)(2,1)}), bf16[256,8,640]{2,0,1:T(8,128)(2,1)}, u32[]{:S(2)}, u32[]{:S(2)}) async-start(bf16[256,8,640]{2,0,1:T(8,128)(2,1)} %broadcast_in_dim.54), calls=%async_computation.2 | async-start | bytes 5242880 | tf_op jit(solution)/shard_map/all_to_all | solution.py:45
  55.5 79.0 %all-gather.2.cloned.1.call-start = ((), (), s32[]{:S(2)}) async-start(), calls=%async_computation.5 | async-start | bytes 2949120 | tf_op jit(solution)/shard_map/all_gather | solution.py:51
  56.3 226.4 %reduce-scatter.3.cloned.1.call-start = ((), (), s32[]{:S(2)}) async-start(), calls=%async_computation.6 | async-start | bytes 2949120 | tf_op jit(solution)/shard_map/reduce_scatter | solution.py:124
  56.3 8.0 %collective-permute-start = (bf16[256,640]{1,0:T(8,128)(2,1)S(1)}, bf16[256,640]{1,0:T(8,128)(2,1)S(1)}, u32[]{:S(2)}, u32[]{:S(2)}) collective-permute-start(bf16[256,640]{1,0:T(8,128)(2,1)S(1)} %copy-done.4), channel_id=1, source_target_pairs={{0,8},{8,0},{1,9},{9,1},{2,10},{10,2},{3,11},{11,3},{4,12},{12,4},... | collective-permute-start | bytes 983048 | tf_op jit(solution)/shard_map/ppermute | solution.py:15
  110.2 7.0 %copy-start = (f32[5,512,2048]{2,1,0:T(8,128)}, f32[5,512,2048]{2,1,0:T(8,128)S(1)}, u32[]{:S(2)}) copy-start(f32[5,512,2048]{2,1,0:T(8,128)S(1)} %get-tuple-element.24) | copy-start | bytes 62914564
  139.0 12.8 %copy-start.3 = (bf16[256,8,640]{0,2,1:T(8,128)(2,1)S(1)}, bf16[256,8,640]{0,2,1:T(8,128)(2,1)}, u32[]{:S(2)}) copy-start(bf16[256,8,640]{0,2,1:T(8,128)(2,1)} %copy.72) | copy-start | bytes 7864324
  151.2 7.6 %collective-permute-start.1 = (f32[256,650]{0,1:T(8,128)}, f32[256,650]{0,1:T(8,128)}, u32[]{:S(2)}, u32[]{:S(2)}) collective-permute-start(f32[256,650]{0,1:T(8,128)} %get-tuple-element.9), channel_id=1, source_target_pairs={{0,8},{8,0},{1,9},{9,1},{2,10},{10,2},{3,11},{11,3},{4,12},{12,4},... | collective-permute-start | bytes 1996808 | tf_op jit(solution)/shard_map/ppermute | solution.py:15
  157.0 1.7 collective-permute-start.3
  161.1 1.3 collective-permute-start.2
  162.3 15.5 %copy-start.2 = (bf16[512,640]{0,1:T(8,128)(2,1)S(1)}, bf16[512,640]{0,1:T(8,128)(2,1)}, u32[]{:S(2)}) copy-start(bf16[512,640]{0,1:T(8,128)(2,1)} %copy.65) | copy-start | bytes 1966084
  189.4 155.6 %reduce-scatter.5.cloned.1.call-start = ((), (), s32[]{:S(2)}) async-start(), calls=%async_computation.7 | async-start | bytes 2949120 | tf_op jit(solution)/shard_map/reduce_scatter | solution.py:127
  210.7 9.1 %copy-start.1 = (bf16[2048,5,128]{0,2,1:T(8,128)(2,1)S(1)}, bf16[2048,5,128]{0,2,1:T(8,128)(2,1)}, u32[]{:S(2)}) copy-start(bf16[2048,5,128]{0,2,1:T(8,128)(2,1)} %reshape_reshape.3) | copy-start | bytes 7864324
  212.4 67.4 %all-to-all-start.1 = ((bf16[256,8,640]{2,0,1:T(8,128)(2,1)}), bf16[256,8,640]{2,0,1:T(8,128)(2,1)}, u32[]{:S(2)}, u32[]{:S(2)}) async-start(bf16[256,8,640]{2,0,1:T(8,128)(2,1)} %bitcast.99), calls=%async_computation.1 | async-start | bytes 5242880 | tf_op jit(solution)/shard_map/all_to_all | solution.py:99
  227.8 2.2 collective-permute-start.4
Sparse Core Ops, SparseCore 0:
  58.0 76.4 all-gather.1
  189.6 90.0 reduce-scatter.2
  282.6 62.3 reduce-scatter.4
